TPU v7x, 32 devices: a whole 2x2x4 slice. The times are simulated.
32 devices in a mesh: space: 16 (over z, y, x), ray: 2 (over core).
Axes of the slice: x: 2, y: 2, z: 4, core: 2. Of those that a mesh axis runs over, the one named last changes fastest.
Arguments:
- positions: float32 [3, 512, 256], P(None, ('space', 'ray')), may hold values from -1 to 1
- spacing: float32 [512, 256], P(('space', 'ray')), may hold values from 0.003 to 0.03
- assign: int32 [512, 8, 1], P(('space', 'ray')), may hold values from 0 to 15; in each aligned block of 128 rows (0 to 127, 128 to 255, ..., all dimensions but the last counted through in order) at most 12 rows name the same one
- depth_rank: int32 [512, 8], P(('space', 'ray')), may hold values from 0 to 7, each once within a row
- pixel_grad: float32 [3, 512], P(None, ('space', 'ray')), may hold values from -96 to 96
- fourier: float32 [3, 128], replicated, may hold values from -4 to 4
- first_weight: bfloat16 [16, 256, 256], P('space'), may hold values from -0.375 to 0.375
- first_bias: float32 [16, 256], P('space'), may hold values from -3 to 3
- second_weight: bfloat16 [16, 256, 256], P('space'), may hold values from -0.375 to 0.375
- second_bias: float32 [16, 256], P('space'), may hold values from -3 to 3
- head_weight: bfloat16 [16, 4, 256], P('space'), may hold values from -0.375 to 0.375
- head_bias: float32 [16, 4], P('space'), may hold values from -3 to 3
Outputs:
- grad_first: float32 [16, 256, 256], P('space', 'ray')
- grad_second: float32 [16, 256, 256], P('space', 'ray')
- grad_head: float32 [16, 4, 256], P('space')
- grad_first_bias: float32 [16, 256], P('space')
- grad_second_bias: float32 [16, 256], P('space')
- grad_head_bias: float32 [16, 4], P('space')
Inputs may be any that keep to these rules, and one draw needn't show every extreme that they name: `assign`: within the segments of one device (aligned blocks of 128 rows in ray order), no partition is named more than 12 times. `depth_rank`: each ray's row names every place 0 to 7 once.
All inputs are finite; a program needn't handle non-finite values.
Results may differ from a plain program's by a relative error of at most 0.0053.
Values sent between devices are 32-bit elements; how exact they have to be, the bound alone decides.
No kernel may reach another device: no remote copies, remote signals or barrier semaphores. Data moves between devices by JAX's collectives and lax.ppermute only.
A program may use at most 64 MiB of HBM per device.

v0:
```python
import jax
import jax.numpy as jnp
from jax import lax
from jax.sharding import PartitionSpec as P

SEG_LEN = 32
SEGS = 8
two_pi = 6.283185307179586


def silu_slope(value):
    gate = jax.nn.sigmoid(value)
    return gate * (1.0 + value * (1.0 - gate))


def turn_sin_cos(turns):
    quarter = jnp.round(turns * 4.0)
    angle = (turns - quarter * 0.25) * two_pi
    square = angle * angle
    sine = angle * (
        1.0
        + square
        * (
            -1.0 / 6.0
            + square * (1.0 / 120.0 + square * (-1.0 / 5040.0 + square * (1.0 / 362880.0)))
        )
    )
    cosine = 1.0 + square * (
        -0.5
        + square
        * (
            1.0 / 24.0
            + square * (-1.0 / 720.0 + square * (1.0 / 40320.0 + square * (-1.0 / 3628800.0)))
        )
    )
    step = quarter - 4.0 * jnp.floor(quarter * 0.25)
    flip = step >= 2.0
    odd = (step == 1.0) | (step == 3.0)
    sin_out = jnp.where(odd, cosine, sine)
    cos_out = jnp.where(odd, sine, cosine)
    sin_out = jnp.where(flip, -sin_out, sin_out)
    cos_out = jnp.where(flip != odd, -cos_out, cos_out)
    return (sin_out, cos_out)


def encode(samples, fourier):
    turns = (
        samples[:, 0, :, None] * fourier[0]
        + samples[:, 1, :, None] * fourier[1]
        + samples[:, 2, :, None] * fourier[2]
    )
    sine, cosine = turn_sin_cos(turns)
    joined = jnp.concatenate([sine, cosine], axis=-1)
    return joined.astype(jnp.bfloat16).reshape(-1, joined.shape[-1])


def network(samples, fourier, params):
    first_weight, first_bias, second_weight, second_bias, head_weight, head_bias = params
    seg_count, length = (samples.shape[0], samples.shape[2])
    encoded = encode(samples, fourier)
    pre_first = jnp.dot(encoded, first_weight, preferred_element_type=jnp.float32) + first_bias
    act_first = jax.nn.silu(pre_first).astype(jnp.bfloat16)
    pre_second = jnp.dot(act_first, second_weight, preferred_element_type=jnp.float32) + second_bias
    act_second = jax.nn.silu(pre_second).astype(jnp.bfloat16)
    head_raw = (
        lax.dot_general(
            act_second, head_weight, (((1,), (1,)), ((), ())), preferred_element_type=jnp.float32
        )
        + head_bias
    )
    head_raw = head_raw.reshape(seg_count, length, 4)
    density = jax.nn.softplus(head_raw[..., 0])
    colour = jax.nn.sigmoid(head_raw[..., 1:])
    optical = density * samples[:, 3, :]
    inclusive = jnp.cumsum(optical, axis=1)
    enter_light = jnp.exp(optical - inclusive)
    leave_light = jnp.exp(-inclusive)
    weight = enter_light - leave_light
    seg_colour = jnp.sum(weight[..., None] * colour, axis=1)
    seg_log = -inclusive[:, -1]
    saved = (
        encoded,
        pre_first,
        act_first,
        pre_second,
        act_second,
        head_raw,
        colour,
        weight,
        leave_light,
    )
    return (seg_colour, seg_log, saved)


def backward(samples, params, saved, up_colour, up_log):
    first_weight, first_bias, second_weight, second_bias, head_weight, head_bias = params
    encoded, pre_first, act_first, pre_second, act_second, head_raw, colour, weight, leave_light = (
        saved
    )
    energy = jnp.sum(colour * up_colour[:, None, :], axis=-1)
    spent = weight * energy
    remaining = jnp.sum(spent, axis=1, keepdims=True) - jnp.cumsum(spent, axis=1)
    grad_optical = leave_light * energy - remaining - up_log[:, None]
    grad_density = grad_optical * samples[:, 3, :] * jax.nn.sigmoid(head_raw[..., 0])
    grad_tint = weight[..., None] * up_colour[:, None, :] * colour * (1.0 - colour)
    grad_raw = (
        jnp.concatenate([grad_density[..., None], grad_tint], axis=-1)
        .reshape(-1, 4)
        .astype(jnp.bfloat16)
    )
    grad_head = lax.dot_general(
        grad_raw, act_second, (((0,), (0,)), ((), ())), preferred_element_type=jnp.float32
    )
    grad_head_bias = jnp.sum(grad_raw.astype(jnp.float32), axis=0)
    back_second = jnp.dot(grad_raw, head_weight, preferred_element_type=jnp.float32)
    delta_second = (back_second * silu_slope(pre_second)).astype(jnp.bfloat16)
    grad_second = lax.dot_general(
        act_first, delta_second, (((0,), (0,)), ((), ())), preferred_element_type=jnp.float32
    )
    grad_second_bias = jnp.sum(delta_second.astype(jnp.float32), axis=0)
    back_first = lax.dot_general(
        delta_second, second_weight, (((1,), (1,)), ((), ())), preferred_element_type=jnp.float32
    )
    delta_first = (back_first * silu_slope(pre_first)).astype(jnp.bfloat16)
    grad_first = lax.dot_general(
        encoded, delta_first, (((0,), (0,)), ((), ())), preferred_element_type=jnp.float32
    )
    grad_first_bias = jnp.sum(delta_first.astype(jnp.float32), axis=0)
    return (grad_first, grad_second, grad_head, grad_first_bias, grad_second_bias, grad_head_bias)


def composite(seg_colour, seg_log, depth_rank, pixel_rows):
    before = (depth_rank[:, None, :] < depth_rank[:, :, None]).astype(jnp.float32)
    prefix = jnp.exp(jnp.sum(before * seg_log[:, None, :], axis=2))
    up_colour = prefix[..., None] * pixel_rows[:, None, :]
    shaded = prefix * jnp.sum(seg_colour * pixel_rows[:, None, :], axis=2)
    up_log = jnp.sum(before * shaded[:, :, None], axis=1)
    return (up_colour, up_log)


def per_device(
    positions,
    spacing,
    assign,
    depth_rank,
    pixel_grad,
    fourier,
    first_weight,
    first_bias,
    second_weight,
    second_bias,
    head_weight,
    head_bias,
):
    groups = lax.axis_size("space")
    ray_count = positions.shape[1]
    total = ray_count * SEGS
    capacity = 3 * total // (2 * groups)
    slot_count = capacity * groups
    owner = assign.reshape(total)
    member = (owner[:, None] == jnp.arange(groups, dtype=jnp.int32)[None, :]).astype(jnp.int32)
    earlier = jnp.cumsum(member, axis=0) - member
    within = jnp.sum(earlier * member, axis=1)
    target = owner * capacity + within
    dispatch = (target[:, None] == jnp.arange(slot_count, dtype=jnp.int32)[None, :]).astype(
        jnp.float32
    )
    seg_pos = jnp.transpose(positions.reshape(3, total, SEG_LEN), (1, 0, 2))
    seg_gap = spacing.reshape(total, 1, SEG_LEN)
    segments = jnp.concatenate([seg_pos, seg_gap], axis=1).reshape(total, 4 * SEG_LEN)
    outgoing = lax.dot_general(
        dispatch,
        segments,
        (((0,), (0,)), ((), ())),
        precision=lax.Precision.HIGHEST,
        preferred_element_type=jnp.float32,
    )
    outgoing = outgoing.reshape(groups, capacity, 4 * SEG_LEN)
    arrived = lax.all_to_all(outgoing, "space", split_axis=0, concat_axis=0, tiled=True)
    samples = arrived.reshape(slot_count, 4, SEG_LEN)
    params = tuple(
        (
            item[0]
            for item in (
                first_weight,
                first_bias,
                second_weight,
                second_bias,
                head_weight,
                head_bias,
            )
        )
    )
    seg_colour, seg_log, saved = network(samples, fourier, params)
    partials = jnp.concatenate([seg_colour.T, seg_log[None, :]], axis=0).reshape(
        4, groups, capacity
    )
    returned = lax.all_to_all(partials, "space", split_axis=1, concat_axis=1, tiled=True).reshape(
        4, slot_count
    )
    mine = lax.dot_general(
        dispatch,
        returned,
        (((1,), (1,)), ((), ())),
        precision=lax.Precision.HIGHEST,
        preferred_element_type=jnp.float32,
    )
    up_colour, up_log = composite(
        mine[:, :3].reshape(ray_count, SEGS, 3),
        mine[:, 3].reshape(ray_count, SEGS),
        depth_rank,
        pixel_grad.T,
    )
    upstream = jnp.concatenate([up_colour.reshape(total, 3), up_log.reshape(total, 1)], axis=1)
    sendback = lax.dot_general(
        upstream,
        dispatch,
        (((0,), (0,)), ((), ())),
        precision=lax.Precision.HIGHEST,
        preferred_element_type=jnp.float32,
    )
    sendback = sendback.reshape(4, groups, capacity)
    received = lax.all_to_all(sendback, "space", split_axis=1, concat_axis=1, tiled=True)
    received = received.reshape(4, slot_count).T
    totals = backward(samples, params, saved, received[:, :3], received[:, 3])
    grad_first, grad_second, grad_head, bias_first, bias_second, bias_head = totals
    replicas = lax.axis_size("ray")
    small = jnp.concatenate([grad_head.reshape(-1), bias_first, bias_second, bias_head], axis=0)
    if replicas & replicas - 1 == 0:
        position = lax.axis_index("ray")
        part_first, part_second = (grad_first, grad_second)
        distance = replicas // 2
        while distance >= 1:
            pairs = [(i, i ^ distance) for i in range(replicas)]
            half = part_first.shape[0] // 2
            upper = position // distance % 2
            keep_first = lax.dynamic_slice_in_dim(part_first, upper * half, half, 0)
            send_first = lax.dynamic_slice_in_dim(part_first, (1 - upper) * half, half, 0)
            keep_second = lax.dynamic_slice_in_dim(part_second, upper * half, half, 0)
            send_second = lax.dynamic_slice_in_dim(part_second, (1 - upper) * half, half, 0)
            got_first, got_second, got_small = lax.ppermute(
                (send_first, send_second, small), "ray", pairs
            )
            part_first = keep_first + got_first
            part_second = keep_second + got_second
            small = small + got_small
            distance //= 2
    else:
        part_first = lax.psum_scatter(grad_first, "ray", scatter_dimension=0, tiled=True)
        part_second = lax.psum_scatter(grad_second, "ray", scatter_dimension=0, tiled=True)
        small = lax.psum(small, "ray")
    heads = grad_head.size
    hidden = bias_first.shape[0]
    small_sums = (
        small[:heads].reshape(grad_head.shape),
        small[heads : heads + hidden],
        small[heads + hidden : heads + 2 * hidden],
        small[heads + 2 * hidden :],
    )
    return (
        part_first[None],
        part_second[None],
        small_sums[0][None],
        small_sums[1][None],
        small_sums[2][None],
        small_sums[3][None],
    )


def solution(mesh):
    placed = (
        P(None, ("space", "ray"), None),
        P(("space", "ray"), None),
        P(("space", "ray"), None, None),
        P(("space", "ray"), None),
        P(None, ("space", "ray")),
        P(),
        P("space", None, None),
        P("space", None),
        P("space", None, None),
        P("space", None),
        P("space", None, None),
        P("space", None),
    )
    return jax.shard_map(
        per_device,
        mesh=mesh,
        in_specs=placed,
        out_specs=(
            P("space", "ray", None),
            P("space", "ray", None),
            P("space", None, None),
            P("space", None),
            P("space", None),
            P("space", None),
        ),
        check_vma=False,
    )
```

profile of v0, /device:TPU:1, one launch (start us, length us, event | category | flops | bytes accessed | tf_op | source)
XLA Modules:
  0.0 90.0 jit_solution(858286756958283039)
XLA Ops:
  0.7 0.8 copy.53
  1.6 0.2 reduce_window_sum.30
  1.8 0.2 select_reduce_fusion
  2.0 0.9 reshape.234
  3.0 0.8 reshape.235
  4.0 0.9 fusion.21
  4.9 7.4 %all-to-all-start = ((f32[16,12,128]{2,1,0:T(8,128)}), f32[16,12,128]{2,1,0:T(8,128)S(1)}, u32[]{:S(2)}, u32[]{:S(2)}) async-start(f32[16,12,128]{2,1,0:T(8,128)} %fusion.21), calls=%async_computation | async-start | bytes 262144 | tf_op jit(solution)/shard_map/all_to_all | solution.py:179
  12.3 0.8 slice_bitcast_fusion.3
  13.1 5.8 %all-to-all-done = f32[16,12,128]{2,1,0:T(8,128)S(1)} async-done(((f32[16,12,128]{2,1,0:T(8,128)}), f32[16,12,128]{2,1,0:T(8,128)S(1)}, u32[]{:S(2)}, u32[]{:S(2)}) %all-to-all-start) | async-done | bytes 98336 | tf_op jit(solution)/shard_map/all_to_all | solution.py:179
  19.0 0.2 reshape.237
  19.2 0.9 %slice_reduce_fusion.2 = (f32[192,32]{1,0:T(8,128)S(1)}, f32[192,32]{1,0:T(8,128)S(1)}, f32[192,32]{1,0:T(8,128)S(1)}, f32[192,1,32]{2,1,0:T(1,128)S(1)}) fusion(f32[192,4,32]{2,1,0:T(4,128)S(1)} %reshape.237), kind=kLoop, calls=%fused_computation.61 | loop fusion | bytes 196608 | tf_op jit(solution)/shard_map/slice | solution.py:48
  20.4 5.6 %fusion.2 = (bf16[6144,128]{1,0:T(8,128)(2,1)S(1)}, bf16[6144,128]{1,0:T(8,128)(2,1)S(1)}) fusion(f32[128]{0:T(128)S(1)} %get-tuple-element.19, f32[6144]{0:T(1024)S(1)} %mul.319, f32[128]{0:T(128)S(1)} %get-tuple-element.20, f32[6144]{0:T(1024)S(1)} %mul.314, f32[128]{0:T(128)S(1)} %get-tuple-element.18, f32[6144]{0:T(1024)S(1)} %mul.309), kind=kLoop, calls=%fused_computation.15 | loop fusion | flops 36175872 | bytes 3220992 | tf_op jit(solution)/shard_map/convert.4
  26.1 4.7 %multiply_convert_fusion.1 = (bf16[6144,256]{1,0:T(8,128)(2,1)S(1)}, f32[6144,256]{1,0:T(8,128)}) fusion(f32[256]{0:T(256)S(1)} %bitcast.134, bf16[1,256,256]{2,1,0:T(8,128)(2,1)} %param.18, bf16[6144,128]{1,0:T(8,128)(2,1)S(1)} %get-tuple-element.13, bf16[6144,128]{1,0:T(8,128)(2,1)S(1)} %get-tuple-element.12), kind=kOutput, calls=%fused_computation.11 | convolution fusion | flops 821035008 | bytes 12715008 | tf_op jit(solution)/shard_map/dot_general | solution.py:61
  30.9 4.4 %multiply_convert_fusion = (bf16[6144,256]{1,0:T(8,128)(2,1)S(1)}, f32[6144,256]{1,0:T(8,128)}) fusion(f32[256]{0:T(256)S(1)} %bitcast.135, bf16[6144,256]{1,0:T(8,128)(2,1)S(1)} %get-tuple-element.21, bf16[1,256,256]{2,1,0:T(8,128)(2,1)S(1)} %copy-done), kind=kOutput, calls=%fused_computation.9 | convolution fusion | flops 814743552 | bytes 12715008 | tf_op jit(solution)/shard_map/dot_general | solution.py:63
  35.3 0.9 %convolution_add_fusion.2 = f32[6144,4]{0,1:T(4,128)S(1)} fusion(bf16[6144,256]{1,0:T(8,128)(2,1)S(1)} %get-tuple-element.23, f32[4]{0:T(128)S(1)} %bitcast.130, bf16[1,4,256]{2,1,0:T(4,128)(2,1)S(1)} %copy-done.6), kind=kOutput, calls=%fused_computation.6 | convolution fusion | flops 12607488 | bytes 3246096 | tf_op jit(solution)/shard_map/dot_general | solution.py:66
  36.2 0.9 %reshape.238 = f32[192,32,4]{1,0,2:T(8,128)} reshape(f32[6144,4]{0,1:T(4,128)S(1)} %convolution_add_fusion.2) | data formatting | bytes 196608 | tf_op jit(solution)/shard_map/reshape | solution.py:71
  37.1 0.9 slice.77
  38.4 1.2 %multiply_reduce_fusion.1 = f32[192,3]{0,1:T(4,128)S(1)} fusion(f32[192,32]{1,0:T(8,128)S(1)} %copy.60, f32[192,32,4]{1,0,2:T(8,128)} %reshape.238), kind=kLoop, calls=%fused_computation.48 | loop fusion | flops 91584 | bytes 100608 | tf_op jit(solution)/shard_map/reduce_sum | solution.py:79
  39.8 0.6 copy.61
  40.4 3.5 %all-to-all-start.1 = ((f32[4,16,12]{2,0,1:T(4,128)}), f32[4,16,12]{2,0,1:T(4,128)S(1)}, u32[]{:S(2)}, u32[]{:S(2)}) async-start(f32[4,16,12]{2,0,1:T(4,128)} %copy.61), calls=%async_computation.1 | async-start | bytes 65536 | tf_op jit(solution)/shard_map/all_to_all | solution.py:198
  43.9 0.7 mul.353
  44.6 0.8 mul.354
  45.4 4.7 %all-to-all-done.1 = f32[4,16,12]{2,0,1:T(4,128)S(1)} async-done(((f32[4,16,12]{2,0,1:T(4,128)}), f32[4,16,12]{2,0,1:T(4,128)S(1)}, u32[]{:S(2)}, u32[]{:S(2)}) %all-to-all-start.1) | async-done | bytes 3104 | tf_op jit(solution)/shard_map/all_to_all | solution.py:198
  50.1 0.6 copy.62
  50.8 0.8 reshape.239
  51.6 0.8 fusion.20
  53.3 0.9 fusion.19
  54.3 0.6 copy.67
  54.9 3.7 %all-to-all-start.2 = ((f32[4,16,12]{2,0,1:T(4,128)}), f32[4,16,12]{2,0,1:T(4,128)S(1)}, u32[]{:S(2)}, u32[]{:S(2)}) async-start(f32[4,16,12]{2,0,1:T(4,128)} %copy.67), calls=%async_computation.2 | async-start | bytes 65536 | tf_op jit(solution)/shard_map/all_to_all | solution.py:223
  58.6 6.0 %all-to-all-done.2 = f32[4,16,12]{2,0,1:T(4,128)S(1)} async-done(((f32[4,16,12]{2,0,1:T(4,128)}), f32[4,16,12]{2,0,1:T(4,128)S(1)}, u32[]{:S(2)}, u32[]{:S(2)}) %all-to-all-start.2) | async-done | bytes 3104 | tf_op jit(solution)/shard_map/all_to_all | solution.py:223
  64.6 0.6 copy.68
  65.2 0.8 reshape.242
  66.1 2.4 %multiply_reduce_fusion = (f32[192,32]{1,0:T(8,128)}, bf16[192,32,3]{1,0,2:T(8,128)(2,1)}) fusion(f32[192,3]{0,1:T(4,128)S(1)} %bitcast.126, f32[192,32,4]{1,0,2:T(8,128)} %reshape.238, f32[192,32]{1,0:T(8,128)S(1)} %copy.60), kind=kLoop, calls=%fused_computation.47 | loop fusion | flops 178176 | bytes 162048 | tf_op jit(solution)/shard_map/reduce_sum | solution.py:100
  68.5 1.0 %copy.69 = f32[192,32]{0,1:T(8,128)S(1)} copy(f32[192,32]{1,0:T(8,128)} %get-tuple-element.9) | data formatting | bytes 49152 | tf_op jit(solution)/shard_map/reduce_sum | solution.py:100
  69.9 1.1 %concatenate.35 = bf16[6144,3]{0,1:T(4,128)(2,1)S(1)} reshape(bf16[192,32,3]{1,0,2:T(8,128)(2,1)} %get-tuple-element.10) | data formatting | bytes 73728 | tf_op jit(solution)/shard_map/concatenate | solution.py:107
  71.0 0.5 convolution_bitcast_fusion
  71.5 0.2 convert_reduce_fusion.2
  71.7 5.2 %convert_reduce_fusion = (f32[256]{0:T(256)S(1)}, bf16[6144,256]{1,0:T(8,128)(2,1)S(1)}) fusion(f32[6144,256]{1,0:T(8,128)} %get-tuple-element.24, bf16[1,4,256]{2,1,0:T(4,128)(2,1)S(1)} %copy-done.6, bf16[6144,3]{0,1:T(4,128)(2,1)S(1)} %concatenate.35, bf16[6144,1]{0,1:T(2,128)(2,1)S(1)} %concatenate.34), kind=kOutput, calls=%fused_computation.7 | convolution fusion | flops 29982464 | bytes 9489408 | tf_op jit(solution)/shard_map/dot_general | solution.py:115
  76.9 1.0 %fusion.56 = f32[256,256]{1,0:T(8,128)S(1)} fusion(bf16[6144,256]{1,0:T(8,128)(2,1)S(1)} %copy-done.13, bf16[6144,256]{1,0:T(8,128)(2,1)S(1)} %get-tuple-element.26), kind=kOutput, calls=%fused_computation.126 | convolution fusion | flops 805306368 | bytes 6553600 | tf_op jit(solution)/shard_map/dot_general | solution.py:117
  78.0 2.8 %convert_reduce_fusion.1 = (f32[256]{0:T(256)S(1)}, bf16[6144,256]{1,0:T(8,128)(2,1)S(1)}) fusion(f32[6144,256]{1,0:T(8,128)S(1)} %bitcast.137, bf16[6144,256]{1,0:T(8,128)(2,1)S(1)} %get-tuple-element.26, bf16[1,256,256]{2,1,0:T(8,128)(2,1)S(1)} %copy-done), kind=kOutput, calls=%fused_computation.8 | convolution fusion | flops 822607616 | bytes 12715008 | tf_op jit(solution)/shard_map/dot_general | solution.py:121
  80.8 4.5 %collective-permute-start.2 = (f32[1540]{0:T(1024)S(1)}, f32[1540]{0:T(1024)S(1)}, u32[]{:S(2)}, u32[]{:S(2)}) collective-permute-start(f32[1540]{0:T(1024)S(1)} %pad_maximum_fusion.6), channel_id=1, source_target_pairs={{0,1},{1,0},{2,3},{3,2},{4,5},{5,4},{6,7},{7,6},{8,9},{9,8},{10,11... | collective-permute-start | bytes 18488 | tf_op jit(solution)/shard_map/ppermute | solution.py:241
  85.4 1.0 %fusion.12 = f32[256,256]{1,0:T(8,128)S(1)} fusion(bf16[6144,256]{1,0:T(8,128)(2,1)S(1)} %get-tuple-element.28, bf16[6144,128]{1,0:T(8,128)(2,1)S(1)} %copy-done.4, bf16[6144,128]{1,0:T(8,128)(2,1)S(1)} %copy-done.2), kind=kOutput, calls=%fused_computation.39 | convolution fusion | flops 811597824 | bytes 6553600 | tf_op jit(solution)/shard_map/dot_general | solution.py:125
  86.4 0.5 collective-permute-start
  87.0 0.6 fusion.54
  87.6 0.6 broadcast_in_dim_reshape.4
  88.2 0.5 slice_bitcast_fusion
  88.7 0.7 add_bitcast_fusion
  89.4 0.7 add_bitcast_fusion.1
  (86 shorter events, 2.8 us)
Async XLA Ops:
  0.6 30.2 %copy-start = (bf16[1,256,256]{2,1,0:T(8,128)(2,1)S(1)}, bf16[1,256,256]{2,1,0:T(8,128)(2,1)}, u32[]{:S(2)}) copy-start(bf16[1,256,256]{2,1,0:T(8,128)(2,1)} %param.20) | copy-start | bytes 393220
  1.8 24.3 %copy-start.10 = (f32[1,256]{1,0:T(1,128)S(1)}, f32[1,256]{1,0:T(1,128)}, u32[]{:S(2)}) copy-start(f32[1,256]{1,0:T(1,128)} %param.19) | copy-start | bytes 3076
  2.0 17.0 %copy-start.9 = (s32[128]{0:T(128)}, s32[128]{0:T(128)S(1)}, u32[]{:S(2)}) copy-start(s32[128]{0:T(128)S(1)} %multiply_add_fusion.2) | copy-start | bytes 1540
  4.9 14.1 %all-to-all-start = ((f32[16,12,128]{2,1,0:T(8,128)}), f32[16,12,128]{2,1,0:T(8,128)S(1)}, u32[]{:S(2)}, u32[]{:S(2)}) async-start(f32[16,12,128]{2,1,0:T(8,128)} %fusion.21), calls=%async_computation | async-start | bytes 262144 | tf_op jit(solution)/shard_map/all_to_all | solution.py:179
  26.1 4.8 %copy-start.1 = (bf16[6144,128]{1,0:T(8,128)(2,1)}, bf16[6144,128]{1,0:T(8,128)(2,1)S(1)}, u32[]{:S(2)}) copy-start(bf16[6144,128]{1,0:T(8,128)(2,1)S(1)} %get-tuple-element.12) | copy-start | bytes 4718596
  26.1 4.8 %copy-start.3 = (bf16[6144,128]{1,0:T(8,128)(2,1)}, bf16[6144,128]{1,0:T(8,128)(2,1)S(1)}, u32[]{:S(2)}) copy-start(bf16[6144,128]{1,0:T(8,128)(2,1)S(1)} %get-tuple-element.13) | copy-start | bytes 4718596
  26.1 4.8 %copy-start.11 = (f32[1,256]{1,0:T(1,128)S(1)}, f32[1,256]{1,0:T(1,128)}, u32[]{:S(2)}) copy-start(f32[1,256]{1,0:T(1,128)} %param.21) | copy-start | bytes 3076
  30.8 4.4 %copy-start.12 = (bf16[6144,256]{1,0:T(8,128)(2,1)}, bf16[6144,256]{1,0:T(8,128)(2,1)S(1)}, u32[]{:S(2)}) copy-start(bf16[6144,256]{1,0:T(8,128)(2,1)S(1)} %get-tuple-element.21) | copy-start | bytes 9437188
  30.9 4.4 %copy-start.6 = (bf16[1,4,256]{2,1,0:T(4,128)(2,1)S(1)}, bf16[1,4,256]{2,1,0:T(4,128)(2,1)}, u32[]{:S(2)}) copy-start(bf16[1,4,256]{2,1,0:T(4,128)(2,1)} %param.22) | copy-start | bytes 6148
  30.9 4.4 %copy-start.7 = (f32[1,4]{1,0:T(1,128)S(1)}, f32[1,4]{1,0:T(1,128)}, u32[]{:S(2)}) copy-start(f32[1,4]{1,0:T(1,128)} %param.23) | copy-start | bytes 52
  35.3 8.7 %copy-start.8 = (f32[3,16]{1,0:T(4,128)S(1)}, f32[3,16]{1,0:T(4,128)}, u32[]{:S(2)}) copy-start(f32[3,16]{1,0:T(4,128)} %param.16) | copy-start | bytes 580
  35.3 17.6 %copy-start.5 = (s32[16,8]{0,1:T(8,128)S(1)}, s32[16,8]{0,1:T(8,128)}, u32[]{:S(2)}) copy-start(s32[16,8]{0,1:T(8,128)} %param.15) | copy-start | bytes 1540
  40.4 9.7 %all-to-all-start.1 = ((f32[4,16,12]{2,0,1:T(4,128)}), f32[4,16,12]{2,0,1:T(4,128)S(1)}, u32[]{:S(2)}, u32[]{:S(2)}) async-start(f32[4,16,12]{2,0,1:T(4,128)} %copy.61), calls=%async_computation.1 | async-start | bytes 65536 | tf_op jit(solution)/shard_map/all_to_all | solution.py:198
  54.9 9.7 %all-to-all-start.2 = ((f32[4,16,12]{2,0,1:T(4,128)}), f32[4,16,12]{2,0,1:T(4,128)S(1)}, u32[]{:S(2)}, u32[]{:S(2)}) async-start(f32[4,16,12]{2,0,1:T(4,128)} %copy.67), calls=%async_computation.2 | async-start | bytes 65536 | tf_op jit(solution)/shard_map/all_to_all | solution.py:223
  71.0 7.0 %slice-start = ((s8[6291456]{0:T(1024)(128)(4,1)}), s8[4194304]{0:T(1024)(128)(4,1)S(1)}, s32[]{:S(2)}) async-start(s8[6291456]{0:T(1024)(128)(4,1)} %bitcast.136), calls=%async_computation.3 | async-start | bytes 8388608
  71.7 5.2 %copy-start.13 = (bf16[6144,256]{1,0:T(8,128)(2,1)S(1)}, bf16[6144,256]{1,0:T(8,128)(2,1)}, u32[]{:S(2)}) copy-start(bf16[6144,256]{1,0:T(8,128)(2,1)} %copy-done.12) | copy-start | bytes 9437188
  71.7 6.2 %slice-start.1 = ((s8[6291456]{0:T(1024)(128)(4,1)}), s8[2097152]{0:T(1024)(128)(4,1)S(1)}, s32[]{:S(2)}) async-start(s8[6291456]{0:T(1024)(128)(4,1)} %bitcast.136), calls=%async_computation.4 | async-start | bytes 4194304
  78.0 7.4 %copy-start.2 = (bf16[6144,128]{1,0:T(8,128)(2,1)S(1)}, bf16[6144,128]{1,0:T(8,128)(2,1)}, u32[]{:S(2)}) copy-start(bf16[6144,128]{1,0:T(8,128)(2,1)} %copy-done.1) | copy-start | bytes 4718596
  78.0 7.4 %copy-start.4 = (bf16[6144,128]{1,0:T(8,128)(2,1)S(1)}, bf16[6144,128]{1,0:T(8,128)(2,1)}, u32[]{:S(2)}) copy-start(bf16[6144,128]{1,0:T(8,128)(2,1)} %copy-done.3) | copy-start | bytes 4718596
  80.8 6.2 %collective-permute-start.2 = (f32[1540]{0:T(1024)S(1)}, f32[1540]{0:T(1024)S(1)}, u32[]{:S(2)}, u32[]{:S(2)}) collective-permute-start(f32[1540]{0:T(1024)S(1)} %pad_maximum_fusion.6), channel_id=1, source_target_pairs={{0,1},{1,0},{2,3},{3,2},{4,5},{5,4},{6,7},{7,6},{8,9},{9,8},{10,11... | collective-permute-start | bytes 18488 | tf_op jit(solution)/shard_map/ppermute | solution.py:241
  85.3 3.4 %collective-permute-start.1 = (f32[128,256]{1,0:T(8,128)S(1)}, f32[128,256]{1,0:T(8,128)S(1)}, u32[]{:S(2)}, u32[]{:S(2)}) collective-permute-start(f32[128,256]{1,0:T(8,128)S(1)} %constant_dynamic-slice_fusion.1), channel_id=1, source_target_pairs={{0,1},{1,0},{2,3},{3,2},{4,5},{5,4},{6,7},{7,6},{8,9},{9,8},{10,11... | collective-permute-start | bytes 393224 | tf_op jit(solution)/shard_map/ppermute | solution.py:241
  86.4 2.9 %collective-permute-start = (f32[128,256]{1,0:T(8,128)S(1)}, f32[128,256]{1,0:T(8,128)S(1)}, u32[]{:S(2)}, u32[]{:S(2)}) collective-permute-start(f32[128,256]{1,0:T(8,128)S(1)} %constant_dynamic-slice_fusion), channel_id=1, source_target_pairs={{0,1},{1,0},{2,3},{3,2},{4,5},{5,4},{6,7},{7,6},{8,9},{9,8},{10,11... | collective-permute-start | bytes 393224 | tf_op jit(solution)/shard_map/ppermute | solution.py:241
where the time goes:
time: 90.9 us; the launch traced here: 90 us
  matrix products  23.1 us (25%)
  starting transfers between devices  19.7 us (22%)
  local copies, waits for them, and re-layouts  17.7 us (19%)
  waiting for transfers between devices  16.6 us (18%)
  other arithmetic  11.7 us (13%)
  between operations  1.15 us (1%)
    all_to_all x1, starting transfers between devices, per_device(): lax.all_to_all(outgoing, 'space', split_axis=0, concat_axis=0, tiled=True)  7.41 us
    all_to_all x1, waiting for transfers between devices, per_device(): lax.all_to_all(sendback, 'space', split_axis=1, concat_axis=1, tiled=True)  6.02 us
    all_to_all x1, waiting for transfers between devices, per_device(): lax.all_to_all(outgoing, 'space', split_axis=0, concat_axis=0, tiled=True)  5.85 us
    another operation x2, other arithmetic  5.68 us
    dot_general x1, matrix products, backward(): jnp.dot(grad_raw, head_weight, preferred_element_type=jnp.float32)  5.17 us
    ppermute x3, starting transfers between devices, per_device(): lax.ppermute((send_first, send_second, small), 'ray', pairs)  5.1 us
    dot_general x1, matrix products, network(): jnp.dot(encoded, first_weight, preferred_element_type=jnp.float32)  4.73 us
    all_to_all x1, waiting for transfers between devices, per_device(): lax.all_to_all(partials, 'space', split_axis=1, concat_axis=1, tiled=True)  4.71 us
  transfers between devices with their start and end apart: 6, of which 3 were waited for; matrix products, arithmetic and copies ran while one was open for 6% of the time, Pallas kernels for 0%

commit v1 on v0

--- a/solution.py
+++ b/solution.py
@@ -220,7 +220,22 @@
         preferred_element_type=jnp.float32,
     )
     sendback = sendback.reshape(4, groups, capacity)
-    received = lax.all_to_all(sendback, "space", split_axis=1, concat_axis=1, tiled=True)
+    later = lax.axis_size("space")
+    back = lax.axis_index("space")
+    front, b_next = (later, back)
+    g_now = sendback.shape[1] // front
+    ready = list(sendback.shape)
+    ready[1] = g_now
+    big = ready[1]
+    ready[1] = big * front
+    received = jnp.zeros(ready, sendback.dtype)
+    for dd in range(front):
+        vec_out = lax.dynamic_slice_in_dim(sendback, (b_next ^ dd) * g_now, g_now, axis=1)
+        if dd:
+            vec_out = lax.ppermute(
+                vec_out, axis_name="space", perm=[(it, it ^ dd) for it in range(front)]
+            )
+        received = lax.dynamic_update_slice_in_dim(received, vec_out, (b_next ^ dd) * big, axis=1)
     received = received.reshape(4, slot_count).T
     totals = backward(samples, params, saved, received[:, :3], received[:, 3])
     grad_first, grad_second, grad_head, bias_first, bias_second, bias_head = totals

time: 90.9 us -> 121 us (1.33)
  starting transfers between devices: 19.7 us -> 41.9 us
  local copies, waits for them, and re-layouts: 17.7 us -> 29 us
  waiting for transfers between devices: 16.6 us -> 10.4 us
  other arithmetic: 11.7 us -> 13.6 us
    ppermute x0 -> x15, starting transfers between devices: none -> 22.9 us  [per_device(): lax.ppermute(vec_out, axis_name='space', perm=[(it, it ^ dd) for it in ra...]
    dynamic_update_slice x0 -> x16, local copies, waits for them, and re-layouts: none -> 9.72 us  [per_device(): lax.dynamic_update_slice_in_dim(received, vec_out, (b_next ^ dd) * big, a...]
    all_to_all x1 -> x0, waiting for transfers between devices: 6.02 us -> none  [per_device(): lax.all_to_all(sendback, 'space', split_axis=1, concat_axis=1, tiled=True)]
    all_to_all x1 -> x0, starting transfers between devices: 3.68 us -> none  [per_device(): lax.all_to_all(sendback, 'space', split_axis=1, concat_axis=1, tiled=True)]
    ppermute x3, starting transfers between devices: 5.1 us -> 8.09 us  [per_device(): lax.ppermute((send_first, send_second, small), 'ray', pairs)]
    unnamed x36 -> x40, local copies, waits for them, and re-layouts: 1.02 us -> 2.6 us
  transfers between devices with their start and end apart: 6 -> 20, of which waited for: 3 -> 2; matrix products, arithmetic and copies ran while one was open for 6% -> 14% of each run, Pallas kernels for 0% -> 0%
where the time goes in v1:
time: 121 us; the launch traced here: 119 us
  starting transfers between devices  41.9 us (35%)
  local copies, waits for them, and re-layouts  29 us (24%)
  matrix products  23.2 us (19%)
  other arithmetic  13.6 us (11%)
  waiting for transfers between devices  10.4 us (9%)
  between operations  1.37 us (1%)
    ppermute x15, starting transfers between devices, per_device(): lax.ppermute(vec_out, axis_name='space', perm=[(it, it ^ dd) for it in ra...  22.9 us
    dynamic_update_slice x16, local copies, waits for them, and re-layouts, per_device(): lax.dynamic_update_slice_in_dim(received, vec_out, (b_next ^ dd) * big, a...  9.72 us
    ppermute x3, starting transfers between devices, per_device(): lax.ppermute((send_first, send_second, small), 'ray', pairs)  8.09 us
    all_to_all x1, starting transfers between devices, per_device(): lax.all_to_all(outgoing, 'space', split_axis=0, concat_axis=0, tiled=True)  7.41 us
    all_to_all x1, waiting for transfers between devices, per_device(): lax.all_to_all(outgoing, 'space', split_axis=0, concat_axis=0, tiled=True)  5.84 us
    another operation x2, other arithmetic  5.68 us
    dot_general x1, matrix products, backward(): jnp.dot(grad_raw, head_weight, preferred_element_type=jnp.float32)  5.17 us
    dot_general x1, matrix products, network(): jnp.dot(encoded, first_weight, preferred_element_type=jnp.float32)  4.72 us
  transfers between devices with their start and end apart: 20, of which 2 were waited for; matrix products, arithmetic and copies ran while one was open for 14% of the time, Pallas kernels for 0%

profile of v1, /device:TPU:1, one launch (start us, length us, event | category | flops | bytes accessed | tf_op | source)
XLA Modules:
  0.0 119.5 jit_solution(9917439147552206857)
XLA Ops:
  0.7 0.8 copy.51
  2.0 0.9 reshape.234
  3.0 0.8 reshape.235
  4.0 0.9 fusion.21
  4.9 7.4 %all-to-all-start = ((f32[16,12,128]{2,1,0:T(8,128)}), f32[16,12,128]{2,1,0:T(8,128)S(1)}, u32[]{:S(2)}, u32[]{:S(2)}) async-start(f32[16,12,128]{2,1,0:T(8,128)} %fusion.21), calls=%async_computation | async-start | bytes 262144 | tf_op jit(solution)/shard_map/all_to_all | solution.py:179
  12.3 0.8 slice_bitcast_fusion.3
  13.1 5.8 %all-to-all-done = f32[16,12,128]{2,1,0:T(8,128)S(1)} async-done(((f32[16,12,128]{2,1,0:T(8,128)}), f32[16,12,128]{2,1,0:T(8,128)S(1)}, u32[]{:S(2)}, u32[]{:S(2)}) %all-to-all-start) | async-done | bytes 98336 | tf_op jit(solution)/shard_map/all_to_all | solution.py:179
  19.2 0.9 slice_reduce_fusion.2
  20.4 5.6 %fusion.2 = (bf16[6144,128]{1,0:T(8,128)(2,1)S(1)}, bf16[6144,128]{1,0:T(8,128)(2,1)S(1)}) fusion(f32[128]{0:T(128)S(1)} %get-tuple-element.35, f32[6144]{0:T(1024)S(1)} %mul.319, f32[128]{0:T(128)S(1)} %get-tuple-element.36, f32[6144]{0:T(1024)S(1)} %mul.314, f32[128]{0:T(128)S(1)} %get-tuple-element.34, f32[6144]{0:T(1024)S(1)} %mul.309), kind=kLoop, calls=%fused_computation.15 | loop fusion | flops 36175872 | bytes 3220992 | tf_op jit(solution)/shard_map/convert.4
  26.1 4.7 %multiply_convert_fusion.1 = (bf16[6144,256]{1,0:T(8,128)(2,1)S(1)}, f32[6144,256]{1,0:T(8,128)}) fusion(f32[256]{0:T(256)S(1)} %bitcast.134, bf16[1,256,256]{2,1,0:T(8,128)(2,1)} %param.18, bf16[6144,128]{1,0:T(8,128)(2,1)S(1)} %get-tuple-element.13, bf16[6144,128]{1,0:T(8,128)(2,1)S(1)} %get-tuple-element.12), kind=kOutput, calls=%fused_computation.11 | convolution fusion | flops 821035008 | bytes 12715008 | tf_op jit(solution)/shard_map/dot_general | solution.py:61
  30.9 4.4 %multiply_convert_fusion = (bf16[6144,256]{1,0:T(8,128)(2,1)S(1)}, f32[6144,256]{1,0:T(8,128)}) fusion(f32[256]{0:T(256)S(1)} %bitcast.135, bf16[6144,256]{1,0:T(8,128)(2,1)S(1)} %get-tuple-element.37, bf16[1,256,256]{2,1,0:T(8,128)(2,1)S(1)} %copy-done), kind=kOutput, calls=%fused_computation.9 | convolution fusion | flops 814743552 | bytes 12715008 | tf_op jit(solution)/shard_map/dot_general | solution.py:63
  35.3 0.9 convolution_add_fusion.2
  36.2 0.9 reshape.238
  37.1 1.5 %slice.77 = f32[192,32,1]{1,0,2:T(8,128)} slice(f32[192,32,4]{1,0,2:T(8,128)} %reshape.238), slice={[0:192], [0:32], [0:1]} | slice | bytes 49152 | tf_op jit(solution)/shard_map/slice | solution.py:72
  38.7 1.0 copy.72
  39.9 1.2 multiply_reduce_fusion.1
  41.9 3.5 %all-to-all-start.1 = ((f32[4,16,12]{2,0,1:T(4,128)}), f32[4,16,12]{2,0,1:T(4,128)S(1)}, u32[]{:S(2)}, u32[]{:S(2)}) async-start(f32[4,16,12]{2,0,1:T(4,128)} %copy.59), calls=%async_computation.1 | async-start | bytes 65536 | tf_op jit(solution)/shard_map/all_to_all | solution.py:198
  46.2 0.8 mul.354
  47.1 4.5 %all-to-all-done.1 = f32[4,16,12]{2,0,1:T(4,128)S(1)} async-done(((f32[4,16,12]{2,0,1:T(4,128)}), f32[4,16,12]{2,0,1:T(4,128)S(1)}, u32[]{:S(2)}, u32[]{:S(2)}) %all-to-all-start.1) | async-done | bytes 3104 | tf_op jit(solution)/shard_map/all_to_all | solution.py:198
  52.3 0.8 reshape.239
  53.1 0.8 fusion.20
  54.8 0.9 fusion.19
  55.8 0.7 constant_dynamic-slice_fusion.1
  57.1 2.1 %collective-permute-start.2 = (f32[4,1,12]{2,1,0:T(1,128)}, f32[4,1,12]{2,1,0:T(1,128)}, u32[]{:S(2)}, u32[]{:S(2)}) collective-permute-start(f32[4,1,12]{2,1,0:T(1,128)} %get-tuple-element.26), channel_id=1, source_target_pairs={{0,6},{2,4},{4,2},{6,0},{8,14},{10,12},{12,10},{14,8},{16,22},{18,... | collective-permute-start | bytes 584 | tf_op jit(solution)/shard_map/ppermute | solution.py:235
  59.5 1.3 %collective-permute-start.4 = (f32[4,1,12]{2,1,0:T(1,128)}, f32[4,1,12]{2,1,0:T(1,128)}, u32[]{:S(2)}, u32[]{:S(2)}) collective-permute-start(f32[4,1,12]{2,1,0:T(1,128)} %get-tuple-element.24), channel_id=1, source_target_pairs={{0,10},{2,8},{4,14},{6,12},{8,2},{10,0},{12,6},{14,4},{16,26},{18,... | collective-permute-start | bytes 584 | tf_op jit(solution)/shard_map/ppermute | solution.py:235
  61.3 0.7 dynamic_update_slice.49
  62.0 2.8 %collective-permute-start.6 = (f32[4,1,12]{2,1,0:T(1,128)}, f32[4,1,12]{2,1,0:T(1,128)}, u32[]{:S(2)}, u32[]{:S(2)}) collective-permute-start(f32[4,1,12]{2,1,0:T(1,128)} %get-tuple-element.22), channel_id=1, source_target_pairs={{0,14},{2,12},{4,10},{6,8},{8,6},{10,4},{12,2},{14,0},{16,30},{18,... | collective-permute-start | bytes 584 | tf_op jit(solution)/shard_map/ppermute | solution.py:235
  64.8 0.7 dynamic_update_slice.50
  65.9 0.7 dynamic_update_slice.51
  66.6 2.2 %collective-permute-start.8 = (f32[4,1,12]{2,1,0:T(1,128)}, f32[4,1,12]{2,1,0:T(1,128)}, u32[]{:S(2)}, u32[]{:S(2)}) collective-permute-start(f32[4,1,12]{2,1,0:T(1,128)} %get-tuple-element.20), channel_id=1, source_target_pairs={{0,18},{2,16},{4,22},{6,20},{8,26},{10,24},{12,30},{14,28},{16,2},... | collective-permute-start | bytes 584 | tf_op jit(solution)/shard_map/ppermute | solution.py:235
  70.7 3.7 %collective-permute-start.10 = (f32[4,1,12]{2,1,0:T(1,128)}, f32[4,1,12]{2,1,0:T(1,128)}, u32[]{:S(2)}, u32[]{:S(2)}) collective-permute-start(f32[4,1,12]{2,1,0:T(1,128)} %get-tuple-element.18), channel_id=1, source_target_pairs={{0,22},{2,20},{4,18},{6,16},{8,30},{10,28},{12,26},{14,24},{16,6},... | collective-permute-start | bytes 584 | tf_op jit(solution)/shard_map/ppermute | solution.py:235
  75.6 0.7 dynamic_update_slice.55
  76.3 2.9 %collective-permute-start.12 = (f32[4,1,12]{2,1,0:T(1,128)}, f32[4,1,12]{2,1,0:T(1,128)}, u32[]{:S(2)}, u32[]{:S(2)}) collective-permute-start(f32[4,1,12]{2,1,0:T(1,128)} %get-tuple-element.16), channel_id=1, source_target_pairs={{0,26},{2,24},{4,30},{6,28},{8,18},{10,16},{12,22},{14,20},{16,10}... | collective-permute-start | bytes 584 | tf_op jit(solution)/shard_map/ppermute | solution.py:235
  80.3 0.7 dynamic_update_slice.57
  81.0 4.7 %collective-permute-start.14 = (f32[4,1,12]{2,1,0:T(1,128)S(1)}, f32[4,1,12]{2,1,0:T(1,128)}, u32[]{:S(2)}, u32[]{:S(2)}) collective-permute-start(f32[4,1,12]{2,1,0:T(1,128)S(1)} %get-tuple-element.14), channel_id=1, source_target_pairs={{0,30},{2,28},{4,26},{6,24},{8,22},{10,20},{12,18},{14,16},{16,14}... | collective-permute-start | bytes 584 | tf_op jit(solution)/shard_map/ppermute | solution.py:235
  85.8 0.7 dynamic_update_slice.59
  87.8 0.7 dynamic_update_slice.62
  88.5 0.7 dynamic_update_slice.63
  89.3 2.4 %multiply_reduce_fusion = (f32[192,32]{1,0:T(8,128)}, bf16[192,32,3]{1,0,2:T(8,128)(2,1)}) fusion(f32[192,3]{0,1:T(4,128)S(1)} %bitcast.126, f32[192,32,4]{1,0,2:T(8,128)} %reshape.238, f32[192,32]{1,0:T(8,128)S(1)} %copy.58), kind=kLoop, calls=%fused_computation.47 | loop fusion | flops 178176 | bytes 162048 | tf_op jit(solution)/shard_map/reduce_sum | solution.py:100
  91.8 1.0 copy.65
  93.1 1.1 concatenate.35
  95.0 5.2 %convert_reduce_fusion = (f32[256]{0:T(256)S(1)}, bf16[6144,256]{1,0:T(8,128)(2,1)S(1)}) fusion(f32[6144,256]{1,0:T(8,128)} %get-tuple-element.40, bf16[1,4,256]{2,1,0:T(4,128)(2,1)S(1)} %copy-done.8, bf16[6144,3]{0,1:T(4,128)(2,1)S(1)} %concatenate.35, bf16[6144,1]{0,1:T(2,128)(2,1)S(1)} %concatenate.34), kind=kOutput, calls=%fused_computation.7 | convolution fusion | flops 29982464 | bytes 9489408 | tf_op jit(solution)/shard_map/dot_general | solution.py:115
  100.2 1.0 fusion.56
  101.3 2.8 %convert_reduce_fusion.1 = (f32[256]{0:T(256)S(1)}, bf16[6144,256]{1,0:T(8,128)(2,1)S(1)}) fusion(f32[6144,256]{1,0:T(8,128)S(1)} %bitcast.137, bf16[6144,256]{1,0:T(8,128)(2,1)S(1)} %get-tuple-element.42, bf16[1,256,256]{2,1,0:T(8,128)(2,1)S(1)} %copy-done), kind=kOutput, calls=%fused_computation.8 | convolution fusion | flops 822607616 | bytes 12715008 | tf_op jit(solution)/shard_map/dot_general | solution.py:121
  104.1 7.5 %collective-permute-start.17 = (f32[1540]{0:T(1024)S(1)}, f32[1540]{0:T(1024)S(1)}, u32[]{:S(2)}, u32[]{:S(2)}) collective-permute-start(f32[1540]{0:T(1024)S(1)} %pad_maximum_fusion.6), channel_id=1, source_target_pairs={{0,1},{1,0},{2,3},{3,2},{4,5},{5,4},{6,7},{7,6},{8,9},{9,8},{10,11... | collective-permute-start | bytes 18488 | tf_op jit(solution)/shard_map/ppermute | solution.py:256
  112.3 1.0 fusion.12
  116.3 1.6 %add_bitcast_fusion = f32[1,128,256]{2,1,0:T(8,128)} fusion(f32[128,256]{1,0:T(8,128)S(1)} %collective-permute-done.16, f32[256,256]{1,0:T(8,128)} %copy-done.5, s32[]{:T(128)S(6)} %select_n.129), kind=kLoop, calls=%fused_computation.52 | loop fusion | flops 32768 | bytes 393220 | tf_op jit(solution)/shard_map/broadcast_in_dim | solution.py:277
  117.9 1.6 %add_bitcast_fusion.1 = f32[1,128,256]{2,1,0:T(8,128)} fusion(f32[128,256]{1,0:T(8,128)S(1)} %collective-permute-done.15, f32[256,256]{1,0:T(8,128)} %copy-done.6, s32[]{:T(128)S(6)} %select_n.129), kind=kLoop, calls=%fused_computation.53 | loop fusion | flops 32768 | bytes 393220 | tf_op jit(solution)/shard_map/broadcast_in_dim | solution.py:276
  (134 shorter events, 16.9 us)
Async XLA Ops:
  0.6 30.2 %copy-start = (bf16[1,256,256]{2,1,0:T(8,128)(2,1)S(1)}, bf16[1,256,256]{2,1,0:T(8,128)(2,1)}, u32[]{:S(2)}) copy-start(bf16[1,256,256]{2,1,0:T(8,128)(2,1)} %param.20) | copy-start | bytes 393220
  1.8 24.3 %copy-start.12 = (f32[1,256]{1,0:T(1,128)S(1)}, f32[1,256]{1,0:T(1,128)}, u32[]{:S(2)}) copy-start(f32[1,256]{1,0:T(1,128)} %param.19) | copy-start | bytes 3076
  2.0 11.1 %copy-start.11 = (s32[128]{0:T(128)}, s32[128]{0:T(128)S(1)}, u32[]{:S(2)}) copy-start(s32[128]{0:T(128)S(1)} %multiply_add_fusion.2) | copy-start | bytes 1540
  4.9 14.1 %all-to-all-start = ((f32[16,12,128]{2,1,0:T(8,128)}), f32[16,12,128]{2,1,0:T(8,128)S(1)}, u32[]{:S(2)}, u32[]{:S(2)}) async-start(f32[16,12,128]{2,1,0:T(8,128)} %fusion.21), calls=%async_computation | async-start | bytes 262144 | tf_op jit(solution)/shard_map/all_to_all | solution.py:179
  26.1 4.8 %copy-start.1 = (bf16[6144,128]{1,0:T(8,128)(2,1)}, bf16[6144,128]{1,0:T(8,128)(2,1)S(1)}, u32[]{:S(2)}) copy-start(bf16[6144,128]{1,0:T(8,128)(2,1)S(1)} %get-tuple-element.12) | copy-start | bytes 4718596
  26.1 4.8 %copy-start.3 = (bf16[6144,128]{1,0:T(8,128)(2,1)}, bf16[6144,128]{1,0:T(8,128)(2,1)S(1)}, u32[]{:S(2)}) copy-start(bf16[6144,128]{1,0:T(8,128)(2,1)S(1)} %get-tuple-element.13) | copy-start | bytes 4718596
  26.1 4.8 %copy-start.13 = (f32[1,256]{1,0:T(1,128)S(1)}, f32[1,256]{1,0:T(1,128)}, u32[]{:S(2)}) copy-start(f32[1,256]{1,0:T(1,128)} %param.21) | copy-start | bytes 3076
  30.8 4.4 %copy-start.14 = (bf16[6144,256]{1,0:T(8,128)(2,1)}, bf16[6144,256]{1,0:T(8,128)(2,1)S(1)}, u32[]{:S(2)}) copy-start(bf16[6144,256]{1,0:T(8,128)(2,1)S(1)} %get-tuple-element.37) | copy-start | bytes 9437188
  30.8 4.4 %copy-start.8 = (bf16[1,4,256]{2,1,0:T(4,128)(2,1)S(1)}, bf16[1,4,256]{2,1,0:T(4,128)(2,1)}, u32[]{:S(2)}) copy-start(bf16[1,4,256]{2,1,0:T(4,128)(2,1)} %param.22) | copy-start | bytes 6148
  30.9 4.4 %copy-start.9 = (f32[1,4]{1,0:T(1,128)S(1)}, f32[1,4]{1,0:T(1,128)}, u32[]{:S(2)}) copy-start(f32[1,4]{1,0:T(1,128)} %param.23) | copy-start | bytes 52
  35.3 10.3 %copy-start.10 = (f32[3,16]{1,0:T(4,128)S(1)}, f32[3,16]{1,0:T(4,128)}, u32[]{:S(2)}) copy-start(f32[3,16]{1,0:T(4,128)} %param.16) | copy-start | bytes 580
  35.3 19.1 %copy-start.7 = (s32[16,8]{0,1:T(8,128)S(1)}, s32[16,8]{0,1:T(8,128)}, u32[]{:S(2)}) copy-start(s32[16,8]{0,1:T(8,128)} %param.15) | copy-start | bytes 1540
  41.9 9.7 %all-to-all-start.1 = ((f32[4,16,12]{2,0,1:T(4,128)}), f32[4,16,12]{2,0,1:T(4,128)S(1)}, u32[]{:S(2)}, u32[]{:S(2)}) async-start(f32[4,16,12]{2,0,1:T(4,128)} %copy.59), calls=%async_computation.1 | async-start | bytes 65536 | tf_op jit(solution)/shard_map/all_to_all | solution.py:198
  56.5 4.3 %collective-permute-start = (f32[4,1,12]{2,1,0:T(1,128)}, f32[4,1,12]{2,1,0:T(1,128)}, u32[]{:S(2)}, u32[]{:S(2)}) collective-permute-start(f32[4,1,12]{2,1,0:T(1,128)} %get-tuple-element.28), channel_id=1, source_target_pairs={{0,2},{2,0},{4,6},{6,4},{8,10},{10,8},{12,14},{14,12},{16,18},{18,... | collective-permute-start | bytes 584 | tf_op jit(solution)/shard_map/ppermute | solution.py:235
  57.0 5.0 %collective-permute-start.1 = (f32[4,1,12]{2,1,0:T(1,128)}, f32[4,1,12]{2,1,0:T(1,128)}, u32[]{:S(2)}, u32[]{:S(2)}) collective-permute-start(f32[4,1,12]{2,1,0:T(1,128)} %get-tuple-element.27), channel_id=1, source_target_pairs={{0,4},{2,6},{4,0},{6,2},{8,12},{10,14},{12,8},{14,10},{16,20},{18,... | collective-permute-start | bytes 584 | tf_op jit(solution)/shard_map/ppermute | solution.py:235
  57.1 8.4 %collective-permute-start.2 = (f32[4,1,12]{2,1,0:T(1,128)}, f32[4,1,12]{2,1,0:T(1,128)}, u32[]{:S(2)}, u32[]{:S(2)}) collective-permute-start(f32[4,1,12]{2,1,0:T(1,128)} %get-tuple-element.26), channel_id=1, source_target_pairs={{0,6},{2,4},{4,2},{6,0},{8,14},{10,12},{12,10},{14,8},{16,22},{18,... | collective-permute-start | bytes 584 | tf_op jit(solution)/shard_map/ppermute | solution.py:235
  59.2 7.4 %collective-permute-start.3 = (f32[4,1,12]{2,1,0:T(1,128)}, f32[4,1,12]{2,1,0:T(1,128)}, u32[]{:S(2)}, u32[]{:S(2)}) collective-permute-start(f32[4,1,12]{2,1,0:T(1,128)} %get-tuple-element.25), channel_id=1, source_target_pairs={{0,8},{2,10},{4,12},{6,14},{8,0},{10,2},{12,4},{14,6},{16,24},{18,... | collective-permute-start | bytes 584 | tf_op jit(solution)/shard_map/ppermute | solution.py:235
  59.5 10.0 %collective-permute-start.4 = (f32[4,1,12]{2,1,0:T(1,128)}, f32[4,1,12]{2,1,0:T(1,128)}, u32[]{:S(2)}, u32[]{:S(2)}) collective-permute-start(f32[4,1,12]{2,1,0:T(1,128)} %get-tuple-element.24), channel_id=1, source_target_pairs={{0,10},{2,8},{4,14},{6,12},{8,2},{10,0},{12,6},{14,4},{16,26},{18,... | collective-permute-start | bytes 584 | tf_op jit(solution)/shard_map/ppermute | solution.py:235
  60.8 9.9 %collective-permute-start.5 = (f32[4,1,12]{2,1,0:T(1,128)}, f32[4,1,12]{2,1,0:T(1,128)}, u32[]{:S(2)}, u32[]{:S(2)}) collective-permute-start(f32[4,1,12]{2,1,0:T(1,128)} %get-tuple-element.23), channel_id=1, source_target_pairs={{0,12},{2,14},{4,8},{6,10},{8,4},{10,6},{12,0},{14,2},{16,28},{18,... | collective-permute-start | bytes 584 | tf_op jit(solution)/shard_map/ppermute | solution.py:235
  62.0 13.1 %collective-permute-start.6 = (f32[4,1,12]{2,1,0:T(1,128)}, f32[4,1,12]{2,1,0:T(1,128)}, u32[]{:S(2)}, u32[]{:S(2)}) collective-permute-start(f32[4,1,12]{2,1,0:T(1,128)} %get-tuple-element.22), channel_id=1, source_target_pairs={{0,14},{2,12},{4,10},{6,8},{8,6},{10,4},{12,2},{14,0},{16,30},{18,... | collective-permute-start | bytes 584 | tf_op jit(solution)/shard_map/ppermute | solution.py:235
  65.5 10.8 %collective-permute-start.7 = (f32[4,1,12]{2,1,0:T(1,128)}, f32[4,1,12]{2,1,0:T(1,128)}, u32[]{:S(2)}, u32[]{:S(2)}) collective-permute-start(f32[4,1,12]{2,1,0:T(1,128)} %get-tuple-element.21), channel_id=1, source_target_pairs={{0,16},{2,18},{4,20},{6,22},{8,24},{10,26},{12,28},{14,30},{16,0},... | collective-permute-start | bytes 584 | tf_op jit(solution)/shard_map/ppermute | solution.py:235
  66.6 13.3 %collective-permute-start.8 = (f32[4,1,12]{2,1,0:T(1,128)}, f32[4,1,12]{2,1,0:T(1,128)}, u32[]{:S(2)}, u32[]{:S(2)}) collective-permute-start(f32[4,1,12]{2,1,0:T(1,128)} %get-tuple-element.20), channel_id=1, source_target_pairs={{0,18},{2,16},{4,22},{6,20},{8,26},{10,24},{12,30},{14,28},{16,2},... | collective-permute-start | bytes 584 | tf_op jit(solution)/shard_map/ppermute | solution.py:235
  69.5 11.5 %collective-permute-start.9 = (f32[4,1,12]{2,1,0:T(1,128)}, f32[4,1,12]{2,1,0:T(1,128)S(1)}, u32[]{:S(2)}, u32[]{:S(2)}) collective-permute-start(f32[4,1,12]{2,1,0:T(1,128)} %get-tuple-element.19), channel_id=1, source_target_pairs={{0,20},{2,22},{4,16},{6,18},{8,28},{10,30},{12,24},{14,26},{16,4},... | collective-permute-start | bytes 584 | tf_op jit(solution)/shard_map/ppermute | solution.py:235
  70.7 15.1 %collective-permute-start.10 = (f32[4,1,12]{2,1,0:T(1,128)}, f32[4,1,12]{2,1,0:T(1,128)}, u32[]{:S(2)}, u32[]{:S(2)}) collective-permute-start(f32[4,1,12]{2,1,0:T(1,128)} %get-tuple-element.18), channel_id=1, source_target_pairs={{0,22},{2,20},{4,18},{6,16},{8,30},{10,28},{12,26},{14,24},{16,6},... | collective-permute-start | bytes 584 | tf_op jit(solution)/shard_map/ppermute | solution.py:235
  75.0 11.4 %collective-permute-start.11 = (f32[4,1,12]{2,1,0:T(1,128)}, f32[4,1,12]{2,1,0:T(1,128)}, u32[]{:S(2)}, u32[]{:S(2)}) collective-permute-start(f32[4,1,12]{2,1,0:T(1,128)} %get-tuple-element.17), channel_id=1, source_target_pairs={{0,24},{2,26},{4,28},{6,30},{8,16},{10,18},{12,20},{14,22},{16,8},... | collective-permute-start | bytes 584 | tf_op jit(solution)/shard_map/ppermute | solution.py:235
  76.3 10.8 %collective-permute-start.12 = (f32[4,1,12]{2,1,0:T(1,128)}, f32[4,1,12]{2,1,0:T(1,128)}, u32[]{:S(2)}, u32[]{:S(2)}) collective-permute-start(f32[4,1,12]{2,1,0:T(1,128)} %get-tuple-element.16), channel_id=1, source_target_pairs={{0,26},{2,24},{4,30},{6,28},{8,18},{10,16},{12,22},{14,20},{16,10}... | collective-permute-start | bytes 584 | tf_op jit(solution)/shard_map/ppermute | solution.py:235
  80.0 7.9 %collective-permute-start.13 = (f32[4,1,12]{2,1,0:T(1,128)S(1)}, f32[4,1,12]{2,1,0:T(1,128)}, u32[]{:S(2)}, u32[]{:S(2)}) collective-permute-start(f32[4,1,12]{2,1,0:T(1,128)S(1)} %get-tuple-element.15), channel_id=1, source_target_pairs={{0,28},{2,30},{4,24},{6,26},{8,20},{10,22},{12,16},{14,18},{16,12}... | collective-permute-start | bytes 584 | tf_op jit(solution)/shard_map/ppermute | solution.py:235
  81.0 7.5 %collective-permute-start.14 = (f32[4,1,12]{2,1,0:T(1,128)S(1)}, f32[4,1,12]{2,1,0:T(1,128)}, u32[]{:S(2)}, u32[]{:S(2)}) collective-permute-start(f32[4,1,12]{2,1,0:T(1,128)S(1)} %get-tuple-element.14), channel_id=1, source_target_pairs={{0,30},{2,28},{4,26},{6,24},{8,22},{10,20},{12,18},{14,16},{16,14}... | collective-permute-start | bytes 584 | tf_op jit(solution)/shard_map/ppermute | solution.py:235
  94.2 7.0 %slice-start = ((s8[6291456]{0:T(1024)(128)(4,1)}), s8[4194304]{0:T(1024)(128)(4,1)S(1)}, s32[]{:S(2)}) async-start(s8[6291456]{0:T(1024)(128)(4,1)} %bitcast.136), calls=%async_computation.2 | async-start | bytes 8388608
  95.0 5.2 %copy-start.15 = (bf16[6144,256]{1,0:T(8,128)(2,1)S(1)}, bf16[6144,256]{1,0:T(8,128)(2,1)}, u32[]{:S(2)}) copy-start(bf16[6144,256]{1,0:T(8,128)(2,1)} %copy-done.14) | copy-start | bytes 9437188
  95.0 6.3 %slice-start.1 = ((s8[6291456]{0:T(1024)(128)(4,1)}), s8[2097152]{0:T(1024)(128)(4,1)S(1)}, s32[]{:S(2)}) async-start(s8[6291456]{0:T(1024)(128)(4,1)} %bitcast.136), calls=%async_computation.3 | async-start | bytes 4194304
  101.2 10.4 %copy-start.5 = (f32[256,256]{1,0:T(8,128)}, f32[256,256]{1,0:T(8,128)S(1)}, u32[]{:S(2)}) copy-start(f32[256,256]{1,0:T(8,128)S(1)} %fusion.56) | copy-start | bytes 786436
  101.2 11.1 %copy-start.2 = (bf16[6144,128]{1,0:T(8,128)(2,1)S(1)}, bf16[6144,128]{1,0:T(8,128)(2,1)}, u32[]{:S(2)}) copy-start(bf16[6144,128]{1,0:T(8,128)(2,1)} %copy-done.1) | copy-start | bytes 4718596
  101.2 11.1 %copy-start.4 = (bf16[6144,128]{1,0:T(8,128)(2,1)S(1)}, bf16[6144,128]{1,0:T(8,128)(2,1)}, u32[]{:S(2)}) copy-start(bf16[6144,128]{1,0:T(8,128)(2,1)} %copy-done.3) | copy-start | bytes 4718596
  104.1 10.5 %collective-permute-start.17 = (f32[1540]{0:T(1024)S(1)}, f32[1540]{0:T(1024)S(1)}, u32[]{:S(2)}, u32[]{:S(2)}) collective-permute-start(f32[1540]{0:T(1024)S(1)} %pad_maximum_fusion.6), channel_id=1, source_target_pairs={{0,1},{1,0},{2,3},{3,2},{4,5},{5,4},{6,7},{7,6},{8,9},{9,8},{10,11... | collective-permute-start | bytes 18488 | tf_op jit(solution)/shard_map/ppermute | solution.py:256
  112.3 4.0 %collective-permute-start.16 = (f32[128,256]{1,0:T(8,128)}, f32[128,256]{1,0:T(8,128)S(1)}, u32[]{:S(2)}, u32[]{:S(2)}) collective-permute-start(f32[128,256]{1,0:T(8,128)} %constant_dynamic-slice_fusion.17), channel_id=1, source_target_pairs={{0,1},{1,0},{2,3},{3,2},{4,5},{5,4},{6,7},{7,6},{8,9},{9,8},{10,11... | collective-permute-start | bytes 393224 | tf_op jit(solution)/shard_map/ppermute | solution.py:256
  113.3 0.7 copy-start.6
  114.1 3.8 %collective-permute-start.15 = (f32[128,256]{1,0:T(8,128)S(1)}, f32[128,256]{1,0:T(8,128)S(1)}, u32[]{:S(2)}, u32[]{:S(2)}) collective-permute-start(f32[128,256]{1,0:T(8,128)S(1)} %constant_dynamic-slice_fusion), channel_id=1, source_target_pairs={{0,1},{1,0},{2,3},{3,2},{4,5},{5,4},{6,7},{7,6},{8,9},{9,8},{10,11... | collective-permute-start | bytes 393224 | tf_op jit(solution)/shard_map/ppermute | solution.py:256
